TPU v7x, 256 devices: a whole 4x4x8 slice. The times are simulated.
256 devices in a mesh: pix: 32 (over z, x), feat: 8 (over y, core).
Axes of the slice: x: 4, y: 4, z: 8, core: 2. Of those that a mesh axis runs over, the one named last changes fastest.
Arguments:
- mass_bin: int32 [262144, 256], P(('pix', 'feat')), may hold values from 0 to 255
- mobility_bin: int32 [262144, 256], P(('pix', 'feat')), may hold values from 0 to 15
- intensity: bfloat16 [262144, 256], P(('pix', 'feat')), may hold values from 10 to 4000, as said below
- basis_init: float32 [262144, 64], P(('pix', 'feat')), may hold values from 0.1 to 1
- profile_init: float32 [64, 4096], P(None, 'feat'), may hold values from 0.1 to 1
Outputs:
- basis: float32 [262144, 64], P(('pix', 'feat'))
- profiles: float32 [64, 4096], P(None, 'feat')
Inputs may be any that keep to these rules, and one draw needn't show every extreme that they name: `intensity`: positive peak intensities.
All inputs are finite; a program needn't handle non-finite values.
Results may differ from a plain program's by a relative error of at most 0.00045.
Values may be sent and summed in bfloat16 or wider, within the bound.
No kernel may reach another device: no remote copies, remote signals or barrier semaphores. Data moves between devices by JAX's collectives and lax.ppermute only.
A program may use at most 64 MiB of HBM per device.

v0:
```python
import math

import jax
import jax.numpy as jnp
from jax import lax
from jax.sharding import PartitionSpec as P

MZ = 256
MOB = 16
PEAKS = 256
ITERS = 2
SIDE = 64


EPS = 1e-06


def bin_block(args):
    mass, mobility, weight = args
    feature = mobility * MZ + mass
    hi = feature // SIDE
    lo = feature % SIDE
    side = jnp.arange(SIDE, dtype=jnp.int32)
    hi_hot = (hi[:, :, None] == side[None, None, :]).astype(jnp.bfloat16) * weight[:, :, None]
    lo_hot = (lo[:, :, None] == side[None, None, :]).astype(jnp.bfloat16)
    dense = jnp.einsum("pkh,pkl->phl", hi_hot, lo_hot, preferred_element_type=jnp.float32)
    return dense.reshape(mass.shape[0], MZ * MOB).astype(jnp.bfloat16)


def pairs(n, s):
    return [(i, i ^ s) for i in range(n)]


def scatter_once(x, g, axis, n):
    j = lax.axis_index(axis)
    w = x.shape[1] // n
    x = jnp.roll(x, -j * w, axis=1)
    acc = jnp.concatenate([x[:, :w], g], axis=1)
    for t in range(1, n):
        send = jnp.concatenate([x[:, t * w : (t + 1) * w], g], axis=1)
        acc = acc + lax.ppermute(send, axis, [(i, (i + t) % n) for i in range(n)])
    return acc[:, :w], acc[:, w:]


CORE_BITS = ((0, 2, 3, 4, 1), (2, 0, 1, 3, 4))


def core_pairs(n_pix, n_feat, s):
    out = []
    for d in range(n_pix * n_feat):
        p, f = divmod(d, n_feat)
        bit = CORE_BITS[f % 2][s]
        out.append((d, (p ^ (1 << bit)) * n_feat + f))
    return out


def halve_sum(x, n_pix, n_feat):
    axes = ("pix", "feat")
    p = lax.axis_index("pix")
    core = lax.axis_index("feat") % 2
    first = jnp.where(core == 0, 1 << CORE_BITS[0][0], 1 << CORE_BITS[1][0])
    half = x.shape[1] // 2
    bit = (p // first) % 2
    keep = lax.dynamic_slice_in_dim(x, bit * half, half, axis=1)
    send = lax.dynamic_slice_in_dim(x, (1 - bit) * half, half, axis=1)
    x = keep + lax.ppermute(send, axes, core_pairs(n_pix, n_feat, 0))
    for s in range(1, len(CORE_BITS[0])):
        x = x + lax.ppermute(x, axes, core_pairs(n_pix, n_feat, s))
    other = lax.ppermute(x, axes, core_pairs(n_pix, n_feat, 0))
    return jnp.where(bit == 1, jnp.concatenate([other, x], axis=1), jnp.concatenate([x, other], axis=1))


def exchange_sum(x, axis, n):
    rows = x.shape[0]
    got = lax.all_to_all(x.reshape(n, rows // n, x.shape[1]), axis, 0, 0, tiled=True)
    total = jnp.sum(got, axis=0)
    back = lax.all_to_all(jnp.broadcast_to(total[None], (n,) + total.shape), axis, 0, 0, tiled=True)
    return back.reshape(rows, x.shape[1])


def double_gather(x, g, axis, n):
    j = lax.axis_index(axis)
    s = 1
    while s < n:
        other, got_g = lax.ppermute((x, g), axis, pairs(n, s))
        bit = (j // s) % 2
        x = jnp.where(bit == 1, jnp.concatenate([other, x], axis=1), jnp.concatenate([x, other], axis=1))
        g = g + got_g
        s *= 2
    return x, g


def local(mass_bin, mobility_bin, intensity, basis_init, profile_init):
    n_pix = lax.psum(1, "pix")
    n_feat = lax.psum(1, "feat")
    rows = mass_bin.shape[0]
    block = math.gcd(rows, 1024)
    count = rows // block
    spectra = lax.map(
        bin_block,
        (
            mass_bin.reshape(count, block, PEAKS),
            mobility_bin.reshape(count, block, PEAKS),
            intensity.reshape(count, block, PEAKS),
        ),
    )
    spectra = spectra.reshape(rows, MZ * MOB)
    highest = lax.Precision.HIGHEST
    basis, profiles = (basis_init, profile_init)
    for step in range(ITERS):
        partial_h = lax.dot_general(
            basis.astype(jnp.bfloat16),
            spectra,
            (((0,), (0,)), ((), ())),
            preferred_element_type=jnp.float32,
        )
        partial_gram = lax.dot_general(
            basis,
            basis,
            (((0,), (0,)), ((), ())),
            precision=highest,
            preferred_element_type=jnp.float32,
        )
        shared, gram_feat = scatter_once(partial_h, partial_gram, "feat", n_feat)
        both = exchange_sum(jnp.concatenate([shared, gram_feat], axis=1), "pix", n_pix)
        width = shared.shape[1]
        numer_h = both[:, :width]
        gram_w = both[:, width:]
        profiles = (
            profiles
            * numer_h
            / (
                jnp.dot(gram_w, profiles, precision=highest, preferred_element_type=jnp.float32)
                + EPS
            )
        )
        local_gram = lax.dot_general(
            profiles,
            profiles,
            (((1,), (1,)), ((), ())),
            precision=highest,
            preferred_element_type=jnp.float32,
        )
        profiles_all, gram_h = double_gather(profiles.astype(jnp.bfloat16), local_gram, "feat", n_feat)
        numer_w = lax.dot_general(
            spectra,
            profiles_all,
            (((1,), (1,)), ((), ())),
            preferred_element_type=jnp.float32,
        )
        basis = (
            basis
            * numer_w
            / (jnp.dot(basis, gram_h, precision=highest, preferred_element_type=jnp.float32) + EPS)
        )
    return (basis, profiles)


def solution(mesh):
    return jax.shard_map(
        local,
        mesh=mesh,
        in_specs=(
            P(("pix", "feat"), None),
            P(("pix", "feat"), None),
            P(("pix", "feat"), None),
            P(("pix", "feat"), None),
            P(None, "feat"),
        ),
        out_specs=(P(("pix", "feat"), None), P(None, "feat")),
        check_vma=False,
    )
```

profile of v0, /device:TPU:16, one launch (start us, length us, event | category | flops | bytes accessed | tf_op | source)
XLA Modules:
  0.0 203.8 jit_solution(8873231308493136634)
XLA Ops:
  0.7 2.5 %add_select_fusion.1 = (s32[1024,256]{1,0:T(8,128)S(1)}, s32[1024,256]{1,0:T(8,128)S(1)}) fusion(s32[1024,256]{1,0:T(8,128)} %param.7, s32[1024,256]{1,0:T(8,128)} %param.8), kind=kLoop, calls=%fused_computation.15 | loop fusion | flops 5505024 | bytes 4194304 | tf_op jit(solution)/shard_map/while/body/eval_jaxpr/jit(floor_divide)/jit(_where)/select_n | solution.py:21
  3.1 21.1 %fusion.7 = bf16[1024,64,64]{2,1,0:T(8,128)(2,1)} fusion(s32[1024,256]{1,0:T(8,128)S(1)} %get-tuple-element.14, s32[1024,256]{1,0:T(8,128)S(1)} %get-tuple-element.13, bf16[1024,256]{1,0:T(8,128)(2,1)} %param.9), kind=kOutput, calls=%fused_computation.8 | convolution fusion | flops 2202009600 | bytes 11010048 | tf_op jit(solution)/shard_map/while/body/eval_jaxpr/pkh,pkl->phl/dot_general | solution.py:26
  24.2 18.4 %copy.7 = bf16[1024,64,64]{0,2,1:T(8,128)(2,1)} copy(bf16[1024,64,64]{2,1,0:T(8,128)(2,1)} %fusion.7) | data formatting | bytes 16777216 | tf_op jit(solution)/shard_map/while/body/eval_jaxpr/convert_element_type | solution.py:27
  42.7 0.4 fusion.59
  43.0 6.1 %convolution_bitcast_fusion = f32[64,4096]{1,0:T(8,128)S(1)} fusion(bf16[1024,4096]{0,1:T(8,128)(2,1)} %bitcast.21, f32[1024,64]{0,1:T(8,128)S(1)} %copy-done), kind=kOutput, calls=%fused_computation.9 | convolution fusion | flops 536936448 | bytes 9699328 | tf_op jit(solution)/shard_map/dot_general | solution.py:111
  49.1 0.2 fusion.16
  49.6 1.4 collective-permute-start.1
  50.9 1.6 collective-permute-start.2
  52.5 1.2 collective-permute-start.3
  53.8 1.7 collective-permute-start.4
  55.5 1.8 collective-permute-start.5
  57.3 1.6 collective-permute-start.6
  58.9 3.3 %collective-permute-done.2 = f32[64,576]{1,0:T(8,128)S(1)} collective-permute-done((f32[64,576]{1,0:T(8,128)S(1)}, f32[64,576]{1,0:T(8,128)S(1)}, u32[]{:S(2)}, u32[]{:S(2)}) %collective-permute-start.2) | collective-permute-done | bytes 147488 | tf_op jit(solution)/shard_map/ppermute | solution.py:41
  62.2 1.6 collective-permute-done.3
  63.9 1.6 collective-permute-done.4
  65.4 2.3 %collective-permute-done.5 = f32[64,576]{1,0:T(8,128)S(1)} collective-permute-done((f32[64,576]{1,0:T(8,128)S(1)}, f32[64,576]{1,0:T(8,128)S(1)}, u32[]{:S(2)}, u32[]{:S(2)}) %collective-permute-start.5) | collective-permute-done | bytes 147488 | tf_op jit(solution)/shard_map/ppermute | solution.py:41
  67.7 0.2 collective-permute-done.6
  68.1 23.1 %all_to_all.20 = f32[32,2,576]{2,1,0:T(2,128)S(1)} all-to-all(f32[32,2,576]{2,1,0:T(2,128)S(1)} %reshape.68), channel_id=1, replica_groups=mesh['pix'=32,'feat'=8] {'pix'}, dimensions={0} | all-to-all | bytes 294912 | tf_op jit(solution)/shard_map/all_to_all | solution.py:75
  91.3 14.1 %all_to_all.21 = f32[32,2,576]{2,1,0:T(2,128)S(1)} all-to-all(f32[32,2,576]{2,1,0:T(2,128)S(1)} %broadcast_in_dim.16), channel_id=1, replica_groups=mesh['pix'=32,'feat'=8] {'pix'}, dimensions={0} | all-to-all | bytes 294912 | tf_op jit(solution)/shard_map/all_to_all | solution.py:77
  105.5 0.1 reshape.69
  105.6 0.3 fusion.57
  106.0 1.2 collective-permute-done.7
  107.3 1.3 collective-permute-start.8
  108.5 0.3 fusion.60
  108.9 1.2 collective-permute-done.10
  110.1 0.8 collective-permute-start.11
  110.9 2.0 collective-permute-done.8
  113.0 1.0 collective-permute-start.9
  114.0 2.7 %collective-permute-start.12 = (f32[64,64]{1,0:T(8,128)S(1)}, f32[64,64]{1,0:T(8,128)S(1)}, u32[]{:S(2)}, u32[]{:S(2)}) collective-permute-start(f32[64,64]{1,0:T(8,128)S(1)} %add.134), channel_id=1, source_target_pairs={{0,4},{1,5},{2,6},{3,7},{4,0},{5,1},{6,2},{7,3},{8,12},{9,13},{10,... | collective-permute-start | bytes 49160 | tf_op jit(solution)/shard_map/ppermute | solution.py:85
  116.7 6.1 %collective-permute-done.12 = f32[64,64]{1,0:T(8,128)S(1)} collective-permute-done((f32[64,64]{1,0:T(8,128)S(1)}, f32[64,64]{1,0:T(8,128)S(1)}, u32[]{:S(2)}, u32[]{:S(2)}) %collective-permute-start.12) | collective-permute-done | bytes 16416 | tf_op jit(solution)/shard_map/ppermute | solution.py:85
  122.8 0.4 fusion.10
  123.3 5.2 %fusion.12 = f32[1024,64]{0,1:T(8,128)S(1)} fusion(f32[1024,64]{0,1:T(8,128)S(1)} %fusion.10, f32[1024,64]{0,1:T(8,128)S(1)} %copy-done, bf16[1024,4096]{0,1:T(8,128)(2,1)} %bitcast.22, bf16[64,2048]{1,0:T(8,128)(2,1)S(1)} %maximum_select_fusion.4, bf16[64,2048]{1,0:T(8,128)(2,1)S(1)} %collective-permute-done.9, pred[]{:T(512)S(6)} %eq.67), kind=kOutput, calls=%fused_computation.25 | convolution fusion | flops 539361280 | bytes 9699329 | tf_op jit(solution)/shard_map/dot_general | solution.py:145
  128.4 0.3 slice-done.1
  128.8 2.7 %fusion.45 = f32[64,4096]{1,0:T(8,128)S(1)} fusion(bf16[1024,4096]{0,1:T(8,128)(2,1)S(1)} %bitcast.26, f32[1024,64]{0,1:T(8,128)S(1)} %fusion.12), kind=kOutput, calls=%fused_computation.86 | convolution fusion | flops 536936448 | bytes 9699328 | tf_op jit(solution)/shard_map/dot_general | solution.py:111
  131.4 0.4 fusion.61
  131.8 0.2 fusion.15
  132.2 1.3 collective-permute-start.14
  133.5 1.5 collective-permute-start.15
  135.0 1.3 collective-permute-start.16
  136.3 1.1 collective-permute-start.17
  137.5 0.6 collective-permute-done.13
  138.1 0.7 collective-permute-start.18
  138.8 0.5 collective-permute-done.14
  139.3 2.7 %collective-permute-start.19 = (f32[64,576]{1,0:T(8,128)S(1)}, f32[64,576]{1,0:T(8,128)S(1)}, u32[]{:S(2)}, u32[]{:S(2)}) collective-permute-start(f32[64,576]{1,0:T(8,128)S(1)} %get-tuple-element.42), channel_id=1, source_target_pairs={{0,7},{1,0},{2,1},{3,2},{4,3},{5,4},{6,5},{7,6},{8,15},{9,8},{10,9... | collective-permute-start | bytes 442376 | tf_op jit(solution)/shard_map/ppermute | solution.py:41
  142.1 3.2 %collective-permute-done.15 = f32[64,576]{1,0:T(8,128)S(1)} collective-permute-done((f32[64,576]{1,0:T(8,128)S(1)}, f32[64,576]{1,0:T(8,128)S(1)}, u32[]{:S(2)}, u32[]{:S(2)}) %collective-permute-start.15) | collective-permute-done | bytes 147488 | tf_op jit(solution)/shard_map/ppermute | solution.py:41
  145.3 1.2 collective-permute-done.16
  146.5 1.4 collective-permute-done.17
  148.0 1.7 collective-permute-done.18
  149.7 0.7 collective-permute-done.19
  150.6 15.5 %all_to_all.22 = f32[32,2,576]{2,1,0:T(2,128)S(1)} all-to-all(f32[32,2,576]{2,1,0:T(2,128)S(1)} %reshape.70), channel_id=1, replica_groups=mesh['pix'=32,'feat'=8] {'pix'}, dimensions={0} | all-to-all | bytes 294912 | tf_op jit(solution)/shard_map/all_to_all | solution.py:75
  166.2 14.1 %all_to_all.23 = f32[32,2,576]{2,1,0:T(2,128)S(1)} all-to-all(f32[32,2,576]{2,1,0:T(2,128)S(1)} %broadcast_in_dim.17), channel_id=1, replica_groups=mesh['pix'=32,'feat'=8] {'pix'}, dimensions={0} | all-to-all | bytes 294912 | tf_op jit(solution)/shard_map/all_to_all | solution.py:77
  180.3 0.1 reshape.71
  180.4 0.3 fusion.58
  180.8 1.2 collective-permute-done.20
  182.1 1.3 collective-permute-start.21
  183.4 0.3 fusion.62
  183.8 1.2 collective-permute-done.23
  185.0 0.8 collective-permute-start.24
  185.8 2.0 collective-permute-done.21
  187.8 0.9 collective-permute-start.22
  188.9 2.7 %collective-permute-start.25 = (f32[64,64]{1,0:T(8,128)S(1)}, f32[64,64]{1,0:T(8,128)S(1)}, u32[]{:S(2)}, u32[]{:S(2)}) collective-permute-start(f32[64,64]{1,0:T(8,128)S(1)} %add.147), channel_id=1, source_target_pairs={{0,4},{1,5},{2,6},{3,7},{4,0},{5,1},{6,2},{7,3},{8,12},{9,13},{10,... | collective-permute-start | bytes 49160 | tf_op jit(solution)/shard_map/ppermute | solution.py:85
  191.6 6.1 %collective-permute-done.25 = f32[64,64]{1,0:T(8,128)S(1)} collective-permute-done((f32[64,64]{1,0:T(8,128)S(1)}, f32[64,64]{1,0:T(8,128)S(1)}, u32[]{:S(2)}, u32[]{:S(2)}) %collective-permute-start.25) | collective-permute-done | bytes 16416 | tf_op jit(solution)/shard_map/ppermute | solution.py:85
  197.7 0.4 convolution_add_fusion
  198.1 5.7 %fusion.11 = f32[1024,64]{0,1:T(8,128)} fusion(f32[1024,64]{0,1:T(8,128)S(1)} %convolution_add_fusion, f32[1024,64]{0,1:T(8,128)S(1)} %fusion.12, bf16[1024,4096]{0,1:T(8,128)(2,1)} %bitcast.23, bf16[64,2048]{1,0:T(8,128)(2,1)S(1)} %maximum_select_fusion.5, bf16[64,2048]{1,0:T(8,128)(2,1)S(1)} %collective-permute-done.22, pred[]{:T(512)S(6)} %eq.67), kind=kOutput, calls=%fused_computation.23 | convolution fusion | flops 539361280 | bytes 9699329 | tf_op jit(solution)/shard_map/dot_general | solution.py:145
  (42 shorter events, 1.7 us)
Async XLA Ops:
  24.2 18.4 %copy-start = (f32[1024,64]{0,1:T(8,128)S(1)}, f32[1024,64]{0,1:T(8,128)}, u32[]{:S(2)}) copy-start(f32[1024,64]{0,1:T(8,128)} %param.10) | copy-start | bytes 786436
  43.0 62.6 %copy-start.2 = (f32[64,512]{1,0:T(8,128)S(1)}, f32[64,512]{1,0:T(8,128)}, u32[]{:S(2)}) copy-start(f32[64,512]{1,0:T(8,128)} %param.11) | copy-start | bytes 393220
  49.5 6.0 %collective-permute-start = (f32[64,576]{1,0:T(8,128)S(1)}, f32[64,576]{1,0:T(8,128)S(1)}, u32[]{:S(2)}, u32[]{:S(2)}) collective-permute-start(f32[64,576]{1,0:T(8,128)S(1)} %get-tuple-element.43), channel_id=1, source_target_pairs={{0,1},{1,2},{2,3},{3,4},{4,5},{5,6},{6,7},{7,0},{8,9},{9,10},{10,1... | collective-permute-start | bytes 442376 | tf_op jit(solution)/shard_map/ppermute | solution.py:41
  49.6 7.8 %collective-permute-start.1 = (f32[64,576]{1,0:T(8,128)S(1)}, f32[64,576]{1,0:T(8,128)S(1)}, u32[]{:S(2)}, u32[]{:S(2)}) collective-permute-start(f32[64,576]{1,0:T(8,128)S(1)} %get-tuple-element.44), channel_id=1, source_target_pairs={{0,2},{1,3},{2,4},{3,5},{4,6},{5,7},{6,0},{7,1},{8,10},{9,11},{10,... | collective-permute-start | bytes 442376 | tf_op jit(solution)/shard_map/ppermute | solution.py:41
  50.9 11.3 %collective-permute-start.2 = (f32[64,576]{1,0:T(8,128)S(1)}, f32[64,576]{1,0:T(8,128)S(1)}, u32[]{:S(2)}, u32[]{:S(2)}) collective-permute-start(f32[64,576]{1,0:T(8,128)S(1)} %get-tuple-element.45), channel_id=1, source_target_pairs={{0,3},{1,4},{2,5},{3,6},{4,7},{5,0},{6,1},{7,2},{8,11},{9,12},{10,... | collective-permute-start | bytes 442376 | tf_op jit(solution)/shard_map/ppermute | solution.py:41
  52.5 11.3 %collective-permute-start.3 = (f32[64,576]{1,0:T(8,128)S(1)}, f32[64,576]{1,0:T(8,128)S(1)}, u32[]{:S(2)}, u32[]{:S(2)}) collective-permute-start(f32[64,576]{1,0:T(8,128)S(1)} %get-tuple-element.46), channel_id=1, source_target_pairs={{0,4},{1,5},{2,6},{3,7},{4,0},{5,1},{6,2},{7,3},{8,12},{9,13},{10,... | collective-permute-start | bytes 442376 | tf_op jit(solution)/shard_map/ppermute | solution.py:41
  53.8 11.7 %collective-permute-start.4 = (f32[64,576]{1,0:T(8,128)S(1)}, f32[64,576]{1,0:T(8,128)S(1)}, u32[]{:S(2)}, u32[]{:S(2)}) collective-permute-start(f32[64,576]{1,0:T(8,128)S(1)} %get-tuple-element.47), channel_id=1, source_target_pairs={{0,5},{1,6},{2,7},{3,0},{4,1},{5,2},{6,3},{7,4},{8,13},{9,14},{10,... | collective-permute-start | bytes 442376 | tf_op jit(solution)/shard_map/ppermute | solution.py:41
  55.5 12.2 %collective-permute-start.5 = (f32[64,576]{1,0:T(8,128)S(1)}, f32[64,576]{1,0:T(8,128)S(1)}, u32[]{:S(2)}, u32[]{:S(2)}) collective-permute-start(f32[64,576]{1,0:T(8,128)S(1)} %get-tuple-element.48), channel_id=1, source_target_pairs={{0,6},{1,7},{2,0},{3,1},{4,2},{5,3},{6,4},{7,5},{8,14},{9,15},{10,... | collective-permute-start | bytes 442376 | tf_op jit(solution)/shard_map/ppermute | solution.py:41
  57.3 10.6 %collective-permute-start.6 = (f32[64,576]{1,0:T(8,128)S(1)}, f32[64,576]{1,0:T(8,128)S(1)}, u32[]{:S(2)}, u32[]{:S(2)}) collective-permute-start(f32[64,576]{1,0:T(8,128)S(1)} %get-tuple-element.49), channel_id=1, source_target_pairs={{0,7},{1,0},{2,1},{3,2},{4,3},{5,4},{6,5},{7,6},{8,15},{9,8},{10,9... | collective-permute-start | bytes 442376 | tf_op jit(solution)/shard_map/ppermute | solution.py:41
  105.9 1.3 collective-permute-start.7
  107.3 5.6 %collective-permute-start.8 = (bf16[64,1024]{1,0:T(8,128)(2,1)S(1)}, bf16[64,1024]{1,0:T(8,128)(2,1)S(1)}, u32[]{:S(2)}, u32[]{:S(2)}) collective-permute-start(bf16[64,1024]{1,0:T(8,128)(2,1)S(1)} %maximum_select_fusion.6), channel_id=1, source_target_pairs={{0,2},{1,3},{2,0},{3,1},{4,6},{5,7},{6,4},{7,5},{8,10},{9,11},{10,... | collective-permute-start | bytes 393224 | tf_op jit(solution)/shard_map/ppermute | solution.py:85
  108.8 1.3 collective-permute-start.10
  110.1 3.9 %collective-permute-start.11 = (f32[64,64]{1,0:T(8,128)S(1)}, f32[64,64]{1,0:T(8,128)S(1)}, u32[]{:S(2)}, u32[]{:S(2)}) collective-permute-start(f32[64,64]{1,0:T(8,128)S(1)} %add.133), channel_id=1, source_target_pairs={{0,2},{1,3},{2,0},{3,1},{4,6},{5,7},{6,4},{7,5},{8,10},{9,11},{10,... | collective-permute-start | bytes 49160 | tf_op jit(solution)/shard_map/ppermute | solution.py:85
  113.0 10.3 %collective-permute-start.9 = (bf16[64,2048]{1,0:T(8,128)(2,1)S(1)}, bf16[64,2048]{1,0:T(8,128)(2,1)S(1)}, u32[]{:S(2)}, u32[]{:S(2)}) collective-permute-start(bf16[64,2048]{1,0:T(8,128)(2,1)S(1)} %maximum_select_fusion.4), channel_id=1, source_target_pairs={{0,4},{1,5},{2,6},{3,7},{4,0},{5,1},{6,2},{7,3},{8,12},{9,13},{10,... | collective-permute-start | bytes 786440 | tf_op jit(solution)/shard_map/ppermute | solution.py:85
  114.0 8.8 %collective-permute-start.12 = (f32[64,64]{1,0:T(8,128)S(1)}, f32[64,64]{1,0:T(8,128)S(1)}, u32[]{:S(2)}, u32[]{:S(2)}) collective-permute-start(f32[64,64]{1,0:T(8,128)S(1)} %add.134), channel_id=1, source_target_pairs={{0,4},{1,5},{2,6},{3,7},{4,0},{5,1},{6,2},{7,3},{8,12},{9,13},{10,... | collective-permute-start | bytes 49160 | tf_op jit(solution)/shard_map/ppermute | solution.py:85
  122.8 5.6 %slice-start = ((s8[8388608]{0:T(1024)(128)(4,1)}), s8[4194304]{0:T(1024)(128)(4,1)S(1)}, s32[]{:S(2)}) async-start(s8[8388608]{0:T(1024)(128)(4,1)} %bitcast.24), calls=%async_computation.4 | async-start | bytes 8388608
  123.2 5.5 %slice-start.1 = ((s8[8388608]{0:T(1024)(128)(4,1)}), s8[4194304]{0:T(1024)(128)(4,1)S(1)}, s32[]{:S(2)}) async-start(s8[8388608]{0:T(1024)(128)(4,1)} %bitcast.24), calls=%async_computation.5 | async-start | bytes 8388608
  132.2 5.9 %collective-permute-start.13 = (f32[64,576]{1,0:T(8,128)S(1)}, f32[64,576]{1,0:T(8,128)S(1)}, u32[]{:S(2)}, u32[]{:S(2)}) collective-permute-start(f32[64,576]{1,0:T(8,128)S(1)} %get-tuple-element.36), channel_id=1, source_target_pairs={{0,1},{1,2},{2,3},{3,4},{4,5},{5,6},{6,7},{7,0},{8,9},{9,10},{10,1... | collective-permute-start | bytes 442376 | tf_op jit(solution)/shard_map/ppermute | solution.py:41
  132.2 7.1 %collective-permute-start.14 = (f32[64,576]{1,0:T(8,128)S(1)}, f32[64,576]{1,0:T(8,128)S(1)}, u32[]{:S(2)}, u32[]{:S(2)}) collective-permute-start(f32[64,576]{1,0:T(8,128)S(1)} %get-tuple-element.37), channel_id=1, source_target_pairs={{0,2},{1,3},{2,4},{3,5},{4,6},{5,7},{6,0},{7,1},{8,10},{9,11},{10,... | collective-permute-start | bytes 442376 | tf_op jit(solution)/shard_map/ppermute | solution.py:41
  133.5 11.8 %collective-permute-start.15 = (f32[64,576]{1,0:T(8,128)S(1)}, f32[64,576]{1,0:T(8,128)S(1)}, u32[]{:S(2)}, u32[]{:S(2)}) collective-permute-start(f32[64,576]{1,0:T(8,128)S(1)} %get-tuple-element.38), channel_id=1, source_target_pairs={{0,3},{1,4},{2,5},{3,6},{4,7},{5,0},{6,1},{7,2},{8,11},{9,12},{10,... | collective-permute-start | bytes 442376 | tf_op jit(solution)/shard_map/ppermute | solution.py:41
  135.0 11.5 %collective-permute-start.16 = (f32[64,576]{1,0:T(8,128)S(1)}, f32[64,576]{1,0:T(8,128)S(1)}, u32[]{:S(2)}, u32[]{:S(2)}) collective-permute-start(f32[64,576]{1,0:T(8,128)S(1)} %get-tuple-element.39), channel_id=1, source_target_pairs={{0,4},{1,5},{2,6},{3,7},{4,0},{5,1},{6,2},{7,3},{8,12},{9,13},{10,... | collective-permute-start | bytes 442376 | tf_op jit(solution)/shard_map/ppermute | solution.py:41
  136.3 11.6 %collective-permute-start.17 = (f32[64,576]{1,0:T(8,128)S(1)}, f32[64,576]{1,0:T(8,128)S(1)}, u32[]{:S(2)}, u32[]{:S(2)}) collective-permute-start(f32[64,576]{1,0:T(8,128)S(1)} %get-tuple-element.40), channel_id=1, source_target_pairs={{0,5},{1,6},{2,7},{3,0},{4,1},{5,2},{6,3},{7,4},{8,13},{9,14},{10,... | collective-permute-start | bytes 442376 | tf_op jit(solution)/shard_map/ppermute | solution.py:41
  138.1 11.6 %collective-permute-start.18 = (f32[64,576]{1,0:T(8,128)S(1)}, f32[64,576]{1,0:T(8,128)S(1)}, u32[]{:S(2)}, u32[]{:S(2)}) collective-permute-start(f32[64,576]{1,0:T(8,128)S(1)} %get-tuple-element.41), channel_id=1, source_target_pairs={{0,6},{1,7},{2,0},{3,1},{4,2},{5,3},{6,4},{7,5},{8,14},{9,15},{10,... | collective-permute-start | bytes 442376 | tf_op jit(solution)/shard_map/ppermute | solution.py:41
  139.3 11.1 %collective-permute-start.19 = (f32[64,576]{1,0:T(8,128)S(1)}, f32[64,576]{1,0:T(8,128)S(1)}, u32[]{:S(2)}, u32[]{:S(2)}) collective-permute-start(f32[64,576]{1,0:T(8,128)S(1)} %get-tuple-element.42), channel_id=1, source_target_pairs={{0,7},{1,0},{2,1},{3,2},{4,3},{5,4},{6,5},{7,6},{8,15},{9,8},{10,9... | collective-permute-start | bytes 442376 | tf_op jit(solution)/shard_map/ppermute | solution.py:41
  180.7 23.1 %copy-start.1 = (f32[64,512]{1,0:T(8,128)}, f32[64,512]{1,0:T(8,128)S(1)}, u32[]{:S(2)}) copy-start(f32[64,512]{1,0:T(8,128)S(1)} %get-tuple-element.53) | copy-start | bytes 393220
  180.7 1.3 collective-permute-start.20
  182.1 5.6 %collective-permute-start.21 = (bf16[64,1024]{1,0:T(8,128)(2,1)S(1)}, bf16[64,1024]{1,0:T(8,128)(2,1)S(1)}, u32[]{:S(2)}, u32[]{:S(2)}) collective-permute-start(bf16[64,1024]{1,0:T(8,128)(2,1)S(1)} %maximum_select_fusion.7), channel_id=1, source_target_pairs={{0,2},{1,3},{2,0},{3,1},{4,6},{5,7},{6,4},{7,5},{8,10},{9,11},{10,... | collective-permute-start | bytes 393224 | tf_op jit(solution)/shard_map/ppermute | solution.py:85
  183.7 1.3 collective-permute-start.23
  185.0 3.9 %collective-permute-start.24 = (f32[64,64]{1,0:T(8,128)S(1)}, f32[64,64]{1,0:T(8,128)S(1)}, u32[]{:S(2)}, u32[]{:S(2)}) collective-permute-start(f32[64,64]{1,0:T(8,128)S(1)} %add.146), channel_id=1, source_target_pairs={{0,2},{1,3},{2,0},{3,1},{4,6},{5,7},{6,4},{7,5},{8,10},{9,11},{10,... | collective-permute-start | bytes 49160 | tf_op jit(solution)/shard_map/ppermute | solution.py:85
  187.8 10.3 %collective-permute-start.22 = (bf16[64,2048]{1,0:T(8,128)(2,1)S(1)}, bf16[64,2048]{1,0:T(8,128)(2,1)S(1)}, u32[]{:S(2)}, u32[]{:S(2)}) collective-permute-start(bf16[64,2048]{1,0:T(8,128)(2,1)S(1)} %maximum_select_fusion.5), channel_id=1, source_target_pairs={{0,4},{1,5},{2,6},{3,7},{4,0},{5,1},{6,2},{7,3},{8,12},{9,13},{10,... | collective-permute-start | bytes 786440 | tf_op jit(solution)/shard_map/ppermute | solution.py:85
  188.9 8.8 %collective-permute-start.25 = (f32[64,64]{1,0:T(8,128)S(1)}, f32[64,64]{1,0:T(8,128)S(1)}, u32[]{:S(2)}, u32[]{:S(2)}) collective-permute-start(f32[64,64]{1,0:T(8,128)S(1)} %add.147), channel_id=1, source_target_pairs={{0,4},{1,5},{2,6},{3,7},{4,0},{5,1},{6,2},{7,3},{8,12},{9,13},{10,... | collective-permute-start | bytes 49160 | tf_op jit(solution)/shard_map/ppermute | solution.py:85
where the time goes:
time: 205 us; the launch traced here: 204 us
  blocking collectives  66.9 us (33%)
  matrix products  43.3 us (21%)
  waiting for transfers between devices  39.6 us (19%)
  starting transfers between devices  30 us (15%)
  local copies, waits for them, and re-layouts  19.4 us (9%)
  other arithmetic  3.61 us (2%)
    all_to_all x2, blocking collectives, exchange_sum(): lax.all_to_all(x.reshape(n, rows // n, x.shape[1]), axis, 0, 0, tiled=True)  38.7 us
    all_to_all x2, blocking collectives, exchange_sum(): lax.all_to_all(jnp.broadcast_to(total[None], (n,) + total.shape), axis, 0...  28.3 us
    ppermute x12, waiting for transfers between devices, double_gather(): other, got_g = lax.ppermute((x, g), axis, pairs(n, s))  21.1 us
    dot_general x1, matrix products, bin_block(): jnp.einsum('pkh,pkl->phl', hi_hot, lo_hot, preferred_element_type=jnp.flo...  21.1 us
    ppermute x14, waiting for transfers between devices, scatter_once(): acc = acc + lax.ppermute(send, axis, [(i, (i + t) % n) for i in range(n)])  18.4 us
    convert_element_type x1, local copies, waits for them, and re-layouts, bin_block(): return dense.reshape(mass.shape[0], MZ * MOB).astype(jnp.bfloat16)  18.4 us
    ppermute x14, starting transfers between devices, scatter_once(): acc = acc + lax.ppermute(send, axis, [(i, (i + t) % n) for i in range(n)])  18.1 us
    ppermute x12, starting transfers between devices, double_gather(): other, got_g = lax.ppermute((x, g), axis, pairs(n, s))  11.9 us
  transfers between devices with their start and end apart: 26, of which 22 were waited for; matrix products, arithmetic and copies ran while one was open for 1% of the time, Pallas kernels for 0%

commit v1 on v0

--- a/solution.py
+++ b/solution.py
@@ -78,6 +78,14 @@
     return back.reshape(rows, x.shape[1])
 
 
+def exchange_scatter(x, g, axis, n):
+    w = x.shape[1] // n
+    blocks = x.reshape(x.shape[0], n, w).transpose(1, 0, 2)
+    blocks = jnp.concatenate([blocks, jnp.broadcast_to(g[None], (n,) + g.shape)], axis=2)
+    total = jnp.sum(lax.all_to_all(blocks, axis, 0, 0, tiled=True), axis=0)
+    return total[:, :w], total[:, w:]
+
+
 def double_gather(x, g, axis, n):
     j = lax.axis_index(axis)
     s = 1
@@ -121,7 +129,7 @@
             precision=highest,
             preferred_element_type=jnp.float32,
         )
-        shared, gram_feat = scatter_once(partial_h, partial_gram, "feat", n_feat)
+        shared, gram_feat = exchange_scatter(partial_h, partial_gram, "feat", n_feat)
         both = exchange_sum(jnp.concatenate([shared, gram_feat], axis=1), "pix", n_pix)
         width = shared.shape[1]
         numer_h = both[:, :width]

time: 205 us -> 208 us (1.015)
  blocking collectives: 66.9 us -> 107 us
  waiting for transfers between devices: 39.6 us -> 20.8 us
  starting transfers between devices: 30 us -> 12.2 us
    all_to_all x0 -> x2, blocking collectives: none -> 41.2 us  [exchange_scatter(): total = jnp.sum(lax.all_to_all(blocks, axis, 0, 0, tiled=True), axis=0)]
    ppermute x14 -> x0, waiting for transfers between devices: 18.4 us -> none  [scatter_once(): acc = acc + lax.ppermute(send, axis, [(i, (i + t) % n) for i in range(n)])]
    ppermute x14 -> x0, starting transfers between devices: 18.1 us -> none  [scatter_once(): acc = acc + lax.ppermute(send, axis, [(i, (i + t) % n) for i in range(n)])]
  transfers between devices with their start and end apart: 26 -> 12, of which waited for: 22 -> 8; matrix products, arithmetic and copies ran while one was open for 1% -> 1% of each run, Pallas kernels for 0% -> 0%
where the time goes in v1:
time: 208 us; the launch traced here: 206 us
  blocking collectives  107 us (51%)
  matrix products  43.2 us (21%)
  waiting for transfers between devices  20.8 us (10%)
  local copies, waits for them, and re-layouts  19 us (9%)
  starting transfers between devices  12.2 us (6%)
  other arithmetic  3.26 us (2%)
    all_to_all x2, blocking collectives, exchange_scatter(): total = jnp.sum(lax.all_to_all(blocks, axis, 0, 0, tiled=True), axis=0)  41.2 us
    all_to_all x2, blocking collectives, exchange_sum(): lax.all_to_all(x.reshape(n, rows // n, x.shape[1]), axis, 0, 0, tiled=True)  36.8 us
    all_to_all x2, blocking collectives, exchange_sum(): lax.all_to_all(jnp.broadcast_to(total[None], (n,) + total.shape), axis, 0...  28.7 us
    dot_general x1, matrix products, bin_block(): jnp.einsum('pkh,pkl->phl', hi_hot, lo_hot, preferred_element_type=jnp.flo...  21.1 us
    ppermute x12, waiting for transfers between devices, double_gather(): other, got_g = lax.ppermute((x, g), axis, pairs(n, s))  20.8 us
    convert_element_type x1, local copies, waits for them, and re-layouts, bin_block(): return dense.reshape(mass.shape[0], MZ * MOB).astype(jnp.bfloat16)  18.4 us
    ppermute x12, starting transfers between devices, double_gather(): other, got_g = lax.ppermute((x, g), axis, pairs(n, s))  12.2 us
    dot_general x2, matrix products, local(): lax.dot_general(spectra, profiles_all, (((1,), (1,)), ((), ())), preferre...  10.9 us
  transfers between devices with their start and end apart: 12, of which 8 were waited for; matrix products, arithmetic and copies ran while one was open for 1% of the time, Pallas kernels for 0%

profile of v1, /device:TPU:16, one launch (start us, length us, event | category | flops | bytes accessed | tf_op | source)
XLA Modules:
  0.0 206.1 jit_solution(6710742789415376469)
XLA Ops:
  0.6 2.5 %add_select_fusion.1 = (s32[1024,256]{1,0:T(8,128)S(1)}, s32[1024,256]{1,0:T(8,128)S(1)}) fusion(s32[1024,256]{1,0:T(8,128)} %param.5, s32[1024,256]{1,0:T(8,128)} %param.6), kind=kLoop, calls=%fused_computation.10 | loop fusion | flops 5505024 | bytes 4194304 | tf_op jit(solution)/shard_map/while/body/eval_jaxpr/jit(floor_divide)/jit(_where)/select_n | solution.py:21
  3.1 21.1 %fusion.7 = bf16[1024,64,64]{2,1,0:T(8,128)(2,1)} fusion(s32[1024,256]{1,0:T(8,128)S(1)} %get-tuple-element.13, s32[1024,256]{1,0:T(8,128)S(1)} %get-tuple-element.12, bf16[1024,256]{1,0:T(8,128)(2,1)} %param.7), kind=kOutput, calls=%fused_computation.8 | convolution fusion | flops 2202009600 | bytes 11010048 | tf_op jit(solution)/shard_map/while/body/eval_jaxpr/pkh,pkl->phl/dot_general | solution.py:26
  24.2 18.4 %copy.13 = bf16[1024,64,64]{0,2,1:T(8,128)(2,1)} copy(bf16[1024,64,64]{2,1,0:T(8,128)(2,1)} %fusion.7) | data formatting | bytes 16777216 | tf_op jit(solution)/shard_map/while/body/eval_jaxpr/convert_element_type | solution.py:27
  42.6 0.0 copy-done
  42.6 0.4 fusion.42
  43.0 6.0 %fusion.31 = f32[4096,64]{0,1:T(8,128)S(1)} fusion(bf16[1024,4096]{0,1:T(8,128)(2,1)} %bitcast.36, f32[1024,64]{0,1:T(8,128)S(1)} %copy-done), kind=kOutput, calls=%fused_computation.55 | convolution fusion | flops 536936448 | bytes 9699328 | tf_op jit(solution)/shard_map/dot_general | solution.py:119
  49.0 0.1 copy.21
  49.1 0.1 pad_maximum_fusion
  49.2 20.4 %all_to_all.30 = f32[8,64,576]{2,1,0:T(8,128)S(1)} all-to-all(f32[8,64,576]{2,1,0:T(8,128)S(1)} %pad_maximum_fusion), channel_id=1, replica_groups=mesh['pix'=32,'feat'=8] {'feat'}, dimensions={0} | all-to-all | bytes 2359296 | tf_op jit(solution)/shard_map/all_to_all | solution.py:85
  69.6 0.1 reduce_sum.36
  69.7 0.1 reshape.76
  69.8 22.3 %all_to_all.31 = f32[32,2,576]{2,1,0:T(2,128)S(1)} all-to-all(f32[32,2,576]{2,1,0:T(2,128)S(1)} %reshape.76), channel_id=1, replica_groups=mesh['pix'=32,'feat'=8] {'pix'}, dimensions={0} | all-to-all | bytes 294912 | tf_op jit(solution)/shard_map/all_to_all | solution.py:75
  92.1 0.1 reduce_sum.37
  92.2 14.3 %all_to_all.32 = f32[32,2,576]{2,1,0:T(2,128)S(1)} all-to-all(f32[32,2,576]{2,1,0:T(2,128)S(1)} %broadcast_in_dim.21), channel_id=1, replica_groups=mesh['pix'=32,'feat'=8] {'pix'}, dimensions={0} | all-to-all | bytes 294912 | tf_op jit(solution)/shard_map/all_to_all | solution.py:77
  106.5 0.1 reshape.77
  106.7 0.0 copy-done.2
  106.7 0.3 fusion.40
  106.9 0.1 collective-permute-start
  107.0 1.2 collective-permute-done
  108.3 1.8 collective-permute-start.1
  110.1 0.3 fusion.43
  110.4 0.3 collective-permute-start.3
  110.7 1.2 collective-permute-done.3
  111.9 0.3 collective-permute-start.4
  112.2 1.8 collective-permute-done.1
  114.0 0.1 maximum_select_fusion.4
  114.0 3.1 %collective-permute-start.2 = (bf16[64,2048]{1,0:T(8,128)(2,1)S(1)}, bf16[64,2048]{1,0:T(8,128)(2,1)S(1)}, u32[]{:S(2)}, u32[]{:S(2)}) collective-permute-start(bf16[64,2048]{1,0:T(8,128)(2,1)S(1)} %maximum_select_fusion.4), channel_id=1, source_target_pairs={{0,4},{1,5},{2,6},{3,7},{4,0},{5,1},{6,2},{7,3},{8,12},{9,13},{10,... | collective-permute-start | bytes 786440 | tf_op jit(solution)/shard_map/ppermute | solution.py:93
  117.1 0.0 collective-permute-done.4
  117.1 0.6 collective-permute-start.5
  117.8 6.1 %collective-permute-done.5 = f32[64,64]{1,0:T(8,128)S(1)} collective-permute-done((f32[64,64]{1,0:T(8,128)S(1)}, f32[64,64]{1,0:T(8,128)S(1)}, u32[]{:S(2)}, u32[]{:S(2)}) %collective-permute-start.5) | collective-permute-done | bytes 16416 | tf_op jit(solution)/shard_map/ppermute | solution.py:93
  123.9 0.4 fusion.10
  124.3 0.0 slice-start.1
  124.3 0.0 collective-permute-done.2
  124.3 5.2 %fusion.12 = f32[1024,64]{0,1:T(8,128)S(1)} fusion(f32[1024,64]{0,1:T(8,128)S(1)} %fusion.10, f32[1024,64]{0,1:T(8,128)S(1)} %copy-done, bf16[1024,4096]{0,1:T(8,128)(2,1)} %bitcast.37, bf16[64,2048]{1,0:T(8,128)(2,1)S(1)} %maximum_select_fusion.4, bf16[64,2048]{1,0:T(8,128)(2,1)S(1)} %collective-permute-done.2, pred[]{:T(512)S(6)} %eq.65), kind=kOutput, calls=%fused_computation.23 | convolution fusion | flops 539361280 | bytes 9699329 | tf_op jit(solution)/shard_map/dot_general | solution.py:153
  129.5 0.4 fusion.44
  129.9 0.0 slice-done
  129.9 0.0 slice-done.1
  129.9 2.7 %convolution_bitcast_fusion = f32[8,64,512]{2,1,0:T(8,128)S(1)} fusion(bf16[8,512,1024]{2,1,0:T(8,128)(2,1)S(1)} %bitcast.41, f32[1024,64]{0,1:T(8,128)S(1)} %fusion.12), kind=kOutput, calls=%fused_computation.14 | convolution fusion | flops 536936448 | bytes 9699328 | tf_op jit(solution)/shard_map/dot_general | solution.py:119
  132.6 0.1 pad_maximum_fusion.1
  132.7 20.8 %all_to_all.33 = f32[8,64,576]{2,1,0:T(8,128)S(1)} all-to-all(f32[8,64,576]{2,1,0:T(8,128)S(1)} %pad_maximum_fusion.1), channel_id=1, replica_groups=mesh['pix'=32,'feat'=8] {'feat'}, dimensions={0} | all-to-all | bytes 2359296 | tf_op jit(solution)/shard_map/all_to_all | solution.py:85
  153.5 0.1 reduce_sum.38
  153.6 0.1 reshape.78
  153.7 14.5 %all_to_all.34 = f32[32,2,576]{2,1,0:T(2,128)S(1)} all-to-all(f32[32,2,576]{2,1,0:T(2,128)S(1)} %reshape.78), channel_id=1, replica_groups=mesh['pix'=32,'feat'=8] {'pix'}, dimensions={0} | all-to-all | bytes 294912 | tf_op jit(solution)/shard_map/all_to_all | solution.py:75
  168.2 0.1 reduce_sum.39
  168.3 14.4 %all_to_all.35 = f32[32,2,576]{2,1,0:T(2,128)S(1)} all-to-all(f32[32,2,576]{2,1,0:T(2,128)S(1)} %broadcast_in_dim.23), channel_id=1, replica_groups=mesh['pix'=32,'feat'=8] {'pix'}, dimensions={0} | all-to-all | bytes 294912 | tf_op jit(solution)/shard_map/all_to_all | solution.py:77
  182.7 0.1 reshape.79
  182.8 0.3 fusion.41
  183.1 0.0 copy-start.1
  183.1 0.1 collective-permute-start.6
  183.2 1.2 collective-permute-done.6
  184.4 1.8 collective-permute-start.7
  186.2 0.3 fusion.45
  186.5 0.1 collective-permute-start.9
  186.6 1.2 collective-permute-done.9
  187.8 0.3 collective-permute-start.10
  188.1 2.0 collective-permute-done.7
  190.1 0.1 maximum_select_fusion.5
  190.2 3.1 %collective-permute-start.8 = (bf16[64,2048]{1,0:T(8,128)(2,1)S(1)}, bf16[64,2048]{1,0:T(8,128)(2,1)S(1)}, u32[]{:S(2)}, u32[]{:S(2)}) collective-permute-start(bf16[64,2048]{1,0:T(8,128)(2,1)S(1)} %maximum_select_fusion.5), channel_id=1, source_target_pairs={{0,4},{1,5},{2,6},{3,7},{4,0},{5,1},{6,2},{7,3},{8,12},{9,13},{10,... | collective-permute-start | bytes 786440 | tf_op jit(solution)/shard_map/ppermute | solution.py:93
  193.2 0.0 collective-permute-done.10
  193.2 0.6 collective-permute-start.11
  193.9 6.1 %collective-permute-done.11 = f32[64,64]{1,0:T(8,128)S(1)} collective-permute-done((f32[64,64]{1,0:T(8,128)S(1)}, f32[64,64]{1,0:T(8,128)S(1)}, u32[]{:S(2)}, u32[]{:S(2)}) %collective-permute-start.11) | collective-permute-done | bytes 16416 | tf_op jit(solution)/shard_map/ppermute | solution.py:93
  200.0 0.4 convolution_add_fusion
  200.4 0.0 collective-permute-done.8
  200.4 5.7 %fusion.11 = f32[1024,64]{0,1:T(8,128)} fusion(f32[1024,64]{0,1:T(8,128)S(1)} %convolution_add_fusion, f32[1024,64]{0,1:T(8,128)S(1)} %fusion.12, bf16[1024,4096]{0,1:T(8,128)(2,1)} %bitcast.38, bf16[64,2048]{1,0:T(8,128)(2,1)S(1)} %maximum_select_fusion.5, bf16[64,2048]{1,0:T(8,128)(2,1)S(1)} %collective-permute-done.8, pred[]{:T(512)S(6)} %eq.65), kind=kOutput, calls=%fused_computation.21 | convolution fusion | flops 539361280 | bytes 9699329 | tf_op jit(solution)/shard_map/dot_general | solution.py:153
  (15 shorter events, 0.2 us)
Async XLA Ops:
  24.2 18.4 %copy-start = (f32[1024,64]{0,1:T(8,128)S(1)}, f32[1024,64]{0,1:T(8,128)}, u32[]{:S(2)}) copy-start(f32[1024,64]{0,1:T(8,128)} %param.8) | copy-start | bytes 786436
  49.0 57.7 %copy-start.2 = (f32[64,512]{1,0:T(8,128)S(1)}, f32[64,512]{1,0:T(8,128)}, u32[]{:S(2)}) copy-start(f32[64,512]{1,0:T(8,128)} %param.9) | copy-start | bytes 393220
  106.9 1.3 collective-permute-start
  108.3 5.6 %collective-permute-start.1 = (bf16[64,1024]{1,0:T(8,128)(2,1)S(1)}, bf16[64,1024]{1,0:T(8,128)(2,1)S(1)}, u32[]{:S(2)}, u32[]{:S(2)}) collective-permute-start(bf16[64,1024]{1,0:T(8,128)(2,1)S(1)} %maximum_select_fusion.6), channel_id=1, source_target_pairs={{0,2},{1,3},{2,0},{3,1},{4,6},{5,7},{6,4},{7,5},{8,10},{9,11},{10,... | collective-permute-start | bytes 393224 | tf_op jit(solution)/shard_map/ppermute | solution.py:93
  110.4 1.5 collective-permute-start.3
  111.9 5.2 %collective-permute-start.4 = (f32[64,64]{1,0:T(8,128)S(1)}, f32[64,64]{1,0:T(8,128)S(1)}, u32[]{:S(2)}, u32[]{:S(2)}) collective-permute-start(f32[64,64]{1,0:T(8,128)S(1)} %add.76), channel_id=1, source_target_pairs={{0,2},{1,3},{2,0},{3,1},{4,6},{5,7},{6,4},{7,5},{8,10},{9,11},{10,... | collective-permute-start | bytes 49160 | tf_op jit(solution)/shard_map/ppermute | solution.py:93
  114.0 10.3 %collective-permute-start.2 = (bf16[64,2048]{1,0:T(8,128)(2,1)S(1)}, bf16[64,2048]{1,0:T(8,128)(2,1)S(1)}, u32[]{:S(2)}, u32[]{:S(2)}) collective-permute-start(bf16[64,2048]{1,0:T(8,128)(2,1)S(1)} %maximum_select_fusion.4), channel_id=1, source_target_pairs={{0,4},{1,5},{2,6},{3,7},{4,0},{5,1},{6,2},{7,3},{8,12},{9,13},{10,... | collective-permute-start | bytes 786440 | tf_op jit(solution)/shard_map/ppermute | solution.py:93
  117.1 6.7 %collective-permute-start.5 = (f32[64,64]{1,0:T(8,128)S(1)}, f32[64,64]{1,0:T(8,128)S(1)}, u32[]{:S(2)}, u32[]{:S(2)}) collective-permute-start(f32[64,64]{1,0:T(8,128)S(1)} %add.77), channel_id=1, source_target_pairs={{0,4},{1,5},{2,6},{3,7},{4,0},{5,1},{6,2},{7,3},{8,12},{9,13},{10,... | collective-permute-start | bytes 49160 | tf_op jit(solution)/shard_map/ppermute | solution.py:93
  123.9 6.0 %slice-start = ((s8[8388608]{0:T(1024)(128)(4,1)}), s8[4194304]{0:T(1024)(128)(4,1)S(1)}, s32[]{:S(2)}) async-start(s8[8388608]{0:T(1024)(128)(4,1)} %bitcast.39), calls=%async_computation.6 | async-start | bytes 8388608
  124.3 5.6 %slice-start.1 = ((s8[8388608]{0:T(1024)(128)(4,1)}), s8[4194304]{0:T(1024)(128)(4,1)S(1)}, s32[]{:S(2)}) async-start(s8[8388608]{0:T(1024)(128)(4,1)} %bitcast.39), calls=%async_computation.7 | async-start | bytes 8388608
  183.1 23.1 %copy-start.1 = (f32[64,512]{1,0:T(8,128)}, f32[64,512]{1,0:T(8,128)S(1)}, u32[]{:S(2)}) copy-start(f32[64,512]{1,0:T(8,128)S(1)} %get-tuple-element.22) | copy-start | bytes 393220
  183.1 1.3 collective-permute-start.6
  184.4 5.6 %collective-permute-start.7 = (bf16[64,1024]{1,0:T(8,128)(2,1)S(1)}, bf16[64,1024]{1,0:T(8,128)(2,1)S(1)}, u32[]{:S(2)}, u32[]{:S(2)}) collective-permute-start(bf16[64,1024]{1,0:T(8,128)(2,1)S(1)} %maximum_select_fusion.7), channel_id=1, source_target_pairs={{0,2},{1,3},{2,0},{3,1},{4,6},{5,7},{6,4},{7,5},{8,10},{9,11},{10,... | collective-permute-start | bytes 393224 | tf_op jit(solution)/shard_map/ppermute | solution.py:93
  186.5 1.3 collective-permute-start.9
  187.8 5.4 %collective-permute-start.10 = (f32[64,64]{1,0:T(8,128)S(1)}, f32[64,64]{1,0:T(8,128)S(1)}, u32[]{:S(2)}, u32[]{:S(2)}) collective-permute-start(f32[64,64]{1,0:T(8,128)S(1)} %add.82), channel_id=1, source_target_pairs={{0,2},{1,3},{2,0},{3,1},{4,6},{5,7},{6,4},{7,5},{8,10},{9,11},{10,... | collective-permute-start | bytes 49160 | tf_op jit(solution)/shard_map/ppermute | solution.py:93
  190.2 10.3 %collective-permute-start.8 = (bf16[64,2048]{1,0:T(8,128)(2,1)S(1)}, bf16[64,2048]{1,0:T(8,128)(2,1)S(1)}, u32[]{:S(2)}, u32[]{:S(2)}) collective-permute-start(bf16[64,2048]{1,0:T(8,128)(2,1)S(1)} %maximum_select_fusion.5), channel_id=1, source_target_pairs={{0,4},{1,5},{2,6},{3,7},{4,0},{5,1},{6,2},{7,3},{8,12},{9,13},{10,... | collective-permute-start | bytes 786440 | tf_op jit(solution)/shard_map/ppermute | solution.py:93
  193.2 6.8 %collective-permute-start.11 = (f32[64,64]{1,0:T(8,128)S(1)}, f32[64,64]{1,0:T(8,128)S(1)}, u32[]{:S(2)}, u32[]{:S(2)}) collective-permute-start(f32[64,64]{1,0:T(8,128)S(1)} %add.83), channel_id=1, source_target_pairs={{0,4},{1,5},{2,6},{3,7},{4,0},{5,1},{6,2},{7,3},{8,12},{9,13},{10,... | collective-permute-start | bytes 49160 | tf_op jit(solution)/shard_map/ppermute | solution.py:93

commit v2 on v0

--- a/solution.py
+++ b/solution.py
@@ -78,6 +78,19 @@
     return back.reshape(rows, x.shape[1])
 
 
+def exchange_gather(x, axis, n):
+    xs = lax.all_to_all(jnp.broadcast_to(x[None], (n,) + x.shape), axis, 0, 0, tiled=True)
+    return xs.transpose(1, 0, 2).reshape(x.shape[0], n * x.shape[1])
+
+
+def double_sum(x, axis, n):
+    s = 1
+    while s < n:
+        x = x + lax.ppermute(x, axis, pairs(n, s))
+        s *= 2
+    return x
+
+
 def double_gather(x, g, axis, n):
     j = lax.axis_index(axis)
     s = 1
@@ -141,7 +154,8 @@
             precision=highest,
             preferred_element_type=jnp.float32,
         )
-        profiles_all, gram_h = double_gather(profiles.astype(jnp.bfloat16), local_gram, "feat", n_feat)
+        profiles_all = exchange_gather(profiles.astype(jnp.bfloat16), "feat", n_feat)
+        gram_h = double_sum(local_gram, "feat", n_feat)
         numer_w = lax.dot_general(
             spectra,
             profiles_all,

time: 205 us -> 207 us (level)
  waiting for transfers between devices: 39.6 us -> 31.2 us
  starting transfers between devices: 30 us -> 36.2 us
    all_to_all x0 -> x2, starting transfers between devices: none -> 11.8 us  [exchange_gather(): lax.all_to_all(jnp.broadcast_to(x[None], (n,) + x.shape), axis, 0, 0, til...]
    ppermute x12 -> x6, starting transfers between devices: 11.9 us -> 4.5 us  [double_sum(): x = x + lax.ppermute(x, axis, pairs(n, s))]
    ppermute x12 -> x6, waiting for transfers between devices: 21.1 us -> 14 us  [double_sum(): x = x + lax.ppermute(x, axis, pairs(n, s))]
  transfers between devices with their start and end apart: 26 -> 22, of which waited for: 22 -> 13; matrix products, arithmetic and copies ran while one was open for 1% -> 5% of each run, Pallas kernels for 0% -> 0%
where the time goes in v2:
time: 207 us; the launch traced here: 204 us
  blocking collectives  67.7 us (33%)
  matrix products  43.3 us (21%)
  starting transfers between devices  36.2 us (17%)
  waiting for transfers between devices  31.2 us (15%)
  local copies, waits for them, and re-layouts  21.1 us (10%)
  other arithmetic  3.41 us (2%)
    all_to_all x2, blocking collectives, exchange_sum(): lax.all_to_all(x.reshape(n, rows // n, x.shape[1]), axis, 0, 0, tiled=True)  38.4 us
    all_to_all x2, blocking collectives, exchange_sum(): lax.all_to_all(jnp.broadcast_to(total[None], (n,) + total.shape), axis, 0...  29.3 us
    dot_general x1, matrix products, bin_block(): jnp.einsum('pkh,pkl->phl', hi_hot, lo_hot, preferred_element_type=jnp.flo...  21.1 us
    ppermute x14, starting transfers between devices, scatter_once(): acc = acc + lax.ppermute(send, axis, [(i, (i + t) % n) for i in range(n)])  19.9 us
    convert_element_type x1, local copies, waits for them, and re-layouts, bin_block(): return dense.reshape(mass.shape[0], MZ * MOB).astype(jnp.bfloat16)  18.4 us
    ppermute x14, waiting for transfers between devices, scatter_once(): acc = acc + lax.ppermute(send, axis, [(i, (i + t) % n) for i in range(n)])  17.2 us
    ppermute x6, waiting for transfers between devices, double_sum(): x = x + lax.ppermute(x, axis, pairs(n, s))  14 us
    all_to_all x2, starting transfers between devices, exchange_gather(): lax.all_to_all(jnp.broadcast_to(x[None], (n,) + x.shape), axis, 0, 0, til...  11.8 us
  transfers between devices with their start and end apart: 22, of which 13 were waited for; matrix products, arithmetic and copies ran while one was open for 5% of the time, Pallas kernels for 0%

profile of v2, /device:TPU:16, one launch (start us, length us, event | category | flops | bytes accessed | tf_op | source)
XLA Modules:
  0.0 203.9 jit_solution(14625455581390919238)
XLA Ops:
  0.7 2.5 %add_select_fusion.1 = (s32[1024,256]{1,0:T(8,128)S(1)}, s32[1024,256]{1,0:T(8,128)S(1)}) fusion(s32[1024,256]{1,0:T(8,128)} %param.7, s32[1024,256]{1,0:T(8,128)} %param.8), kind=kLoop, calls=%fused_computation.15 | loop fusion | flops 5505024 | bytes 4194304 | tf_op jit(solution)/shard_map/while/body/eval_jaxpr/jit(floor_divide)/jit(_where)/select_n | solution.py:21
  3.1 21.1 %fusion.7 = bf16[1024,64,64]{2,1,0:T(8,128)(2,1)} fusion(s32[1024,256]{1,0:T(8,128)S(1)} %get-tuple-element.14, s32[1024,256]{1,0:T(8,128)S(1)} %get-tuple-element.13, bf16[1024,256]{1,0:T(8,128)(2,1)} %param.9), kind=kOutput, calls=%fused_computation.8 | convolution fusion | flops 2202009600 | bytes 11010048 | tf_op jit(solution)/shard_map/while/body/eval_jaxpr/pkh,pkl->phl/dot_general | solution.py:26
  24.2 18.4 %copy.8 = bf16[1024,64,64]{0,2,1:T(8,128)(2,1)} copy(bf16[1024,64,64]{2,1,0:T(8,128)(2,1)} %fusion.7) | data formatting | bytes 16777216 | tf_op jit(solution)/shard_map/while/body/eval_jaxpr/convert_element_type | solution.py:27
  42.7 0.4 fusion.45
  43.1 6.1 %convolution_bitcast_fusion = f32[64,4096]{1,0:T(8,128)S(1)} fusion(bf16[1024,4096]{0,1:T(8,128)(2,1)} %bitcast.31, f32[1024,64]{0,1:T(8,128)S(1)} %copy-done), kind=kOutput, calls=%fused_computation.9 | convolution fusion | flops 536936448 | bytes 9699328 | tf_op jit(solution)/shard_map/dot_general | solution.py:124
  49.1 0.2 fusion.16
  49.3 0.1 fusion.42
  49.4 0.1 pad_maximum_fusion.6
  49.6 1.4 collective-permute-start.1
  50.9 1.6 collective-permute-start.2
  52.6 1.2 collective-permute-start.3
  53.8 1.7 collective-permute-start.4
  55.5 1.8 collective-permute-start.5
  57.3 1.6 collective-permute-start.6
  58.9 3.3 %collective-permute-done.2 = f32[64,576]{1,0:T(8,128)S(1)} collective-permute-done((f32[64,576]{1,0:T(8,128)S(1)}, f32[64,576]{1,0:T(8,128)S(1)}, u32[]{:S(2)}, u32[]{:S(2)}) %collective-permute-start.2) | collective-permute-done | bytes 147488 | tf_op jit(solution)/shard_map/ppermute | solution.py:41
  62.3 1.6 collective-permute-done.3
  63.9 1.6 collective-permute-done.4
  65.4 2.2 %collective-permute-done.5 = f32[64,576]{1,0:T(8,128)S(1)} collective-permute-done((f32[64,576]{1,0:T(8,128)S(1)}, f32[64,576]{1,0:T(8,128)S(1)}, u32[]{:S(2)}, u32[]{:S(2)}) %collective-permute-start.5) | collective-permute-done | bytes 147488 | tf_op jit(solution)/shard_map/ppermute | solution.py:41
  67.7 0.2 collective-permute-done.6
  68.0 0.1 reshape.78
  68.1 23.1 %all_to_all.30 = f32[32,2,576]{2,1,0:T(2,128)S(1)} all-to-all(f32[32,2,576]{2,1,0:T(2,128)S(1)} %reshape.78), channel_id=1, replica_groups=mesh['pix'=32,'feat'=8] {'pix'}, dimensions={0} | all-to-all | bytes 294912 | tf_op jit(solution)/shard_map/all_to_all | solution.py:75
  91.4 14.1 %all_to_all.31 = f32[32,2,576]{2,1,0:T(2,128)S(1)} all-to-all(f32[32,2,576]{2,1,0:T(2,128)S(1)} %broadcast_in_dim.20), channel_id=1, replica_groups=mesh['pix'=32,'feat'=8] {'pix'}, dimensions={0} | all-to-all | bytes 294912 | tf_op jit(solution)/shard_map/all_to_all | solution.py:77
  105.5 0.1 reshape.79
  105.6 0.3 fusion.43
  105.9 0.9 broadcast_in_dim.21
  106.7 4.8 %all-to-all-start.2 = ((bf16[8,64,512]{2,1,0:T(8,128)(2,1)}), bf16[8,64,512]{2,1,0:T(8,128)(2,1)S(1)}, u32[]{:S(2)}, u32[]{:S(2)}) async-start(bf16[8,64,512]{2,1,0:T(8,128)(2,1)} %broadcast_in_dim.21), calls=%async_computation.2 | async-start | bytes 1048576 | tf_op jit(solution)/shard_map/all_to_all | solution.py:82
  111.5 0.3 fusion.46
  111.8 0.2 collective-permute-start.7
  112.0 1.1 collective-permute-done.7
  113.1 1.2 collective-permute-start.8
  114.3 6.0 %collective-permute-done.8 = f32[64,64]{1,0:T(8,128)S(1)} collective-permute-done((f32[64,64]{1,0:T(8,128)S(1)}, f32[64,64]{1,0:T(8,128)S(1)}, u32[]{:S(2)}, u32[]{:S(2)}) %collective-permute-start.8) | collective-permute-done | bytes 16416 | tf_op jit(solution)/shard_map/ppermute | solution.py:89
  120.2 0.9 collective-permute-start.9
  121.2 5.1 %convolution_multiply_fusion.1 = f32[1024,64]{0,1:T(8,128)S(1)} fusion(f32[1024,64]{0,1:T(8,128)S(1)} %copy-done, bf16[64,4096]{1,0:T(8,128)(2,1)S(1)} %bitcast.38, bf16[1024,4096]{0,1:T(8,128)(2,1)} %bitcast.32), kind=kOutput, calls=%fused_computation.25 | convolution fusion | flops 536936448 | bytes 9437184 | tf_op jit(solution)/shard_map/dot_general | solution.py:159
  126.3 0.4 fusion.12
  126.7 0.2 slice-done.1
  127.0 2.7 %fusion.33 = f32[64,4096]{1,0:T(8,128)S(1)} fusion(bf16[1024,4096]{0,1:T(8,128)(2,1)S(1)} %bitcast.36, f32[1024,64]{0,1:T(8,128)S(1)} %fusion.12), kind=kOutput, calls=%fused_computation.68 | convolution fusion | flops 536936448 | bytes 9699328 | tf_op jit(solution)/shard_map/dot_general | solution.py:124
  129.6 0.4 fusion.47
  130.0 0.2 fusion.15
  130.3 0.1 pad_maximum_fusion.14
  130.4 1.0 collective-permute-start.11
  131.5 2.5 %collective-permute-start.12 = (f32[64,576]{1,0:T(8,128)S(1)}, f32[64,576]{1,0:T(8,128)S(1)}, u32[]{:S(2)}, u32[]{:S(2)}) collective-permute-start(f32[64,576]{1,0:T(8,128)S(1)} %get-tuple-element.38), channel_id=1, source_target_pairs={{0,3},{1,4},{2,5},{3,6},{4,7},{5,0},{6,1},{7,2},{8,11},{9,12},{10,... | collective-permute-start | bytes 442376 | tf_op jit(solution)/shard_map/ppermute | solution.py:41
  134.0 0.3 collective-permute-start.13
  134.3 2.6 %collective-permute-start.14 = (f32[64,576]{1,0:T(8,128)S(1)}, f32[64,576]{1,0:T(8,128)S(1)}, u32[]{:S(2)}, u32[]{:S(2)}) collective-permute-start(f32[64,576]{1,0:T(8,128)S(1)} %get-tuple-element.40), channel_id=1, source_target_pairs={{0,5},{1,6},{2,7},{3,0},{4,1},{5,2},{6,3},{7,4},{8,13},{9,14},{10,... | collective-permute-start | bytes 442376 | tf_op jit(solution)/shard_map/ppermute | solution.py:41
  137.0 1.8 collective-permute-start.15
  138.8 2.2 %collective-permute-start.16 = (f32[64,576]{1,0:T(8,128)S(1)}, f32[64,576]{1,0:T(8,128)S(1)}, u32[]{:S(2)}, u32[]{:S(2)}) collective-permute-start(f32[64,576]{1,0:T(8,128)S(1)} %get-tuple-element.42), channel_id=1, source_target_pairs={{0,7},{1,0},{2,1},{3,2},{4,3},{5,4},{6,5},{7,6},{8,15},{9,8},{10,9... | collective-permute-start | bytes 442376 | tf_op jit(solution)/shard_map/ppermute | solution.py:41
  141.0 3.2 %collective-permute-done.12 = f32[64,576]{1,0:T(8,128)S(1)} collective-permute-done((f32[64,576]{1,0:T(8,128)S(1)}, f32[64,576]{1,0:T(8,128)S(1)}, u32[]{:S(2)}, u32[]{:S(2)}) %collective-permute-start.12) | collective-permute-done | bytes 147488 | tf_op jit(solution)/shard_map/ppermute | solution.py:41
  144.2 1.2 collective-permute-done.13
  145.5 0.5 collective-permute-done.14
  146.0 3.2 %collective-permute-done.15 = f32[64,576]{1,0:T(8,128)S(1)} collective-permute-done((f32[64,576]{1,0:T(8,128)S(1)}, f32[64,576]{1,0:T(8,128)S(1)}, u32[]{:S(2)}, u32[]{:S(2)}) %collective-permute-start.15) | collective-permute-done | bytes 147488 | tf_op jit(solution)/shard_map/ppermute | solution.py:41
  149.2 0.1 reshape.81
  149.3 15.3 %all_to_all.32 = f32[32,2,576]{2,1,0:T(2,128)S(1)} all-to-all(f32[32,2,576]{2,1,0:T(2,128)S(1)} %reshape.81), channel_id=1, replica_groups=mesh['pix'=32,'feat'=8] {'pix'}, dimensions={0} | all-to-all | bytes 294912 | tf_op jit(solution)/shard_map/all_to_all | solution.py:75
  164.8 15.1 %all_to_all.33 = f32[32,2,576]{2,1,0:T(2,128)S(1)} all-to-all(f32[32,2,576]{2,1,0:T(2,128)S(1)} %broadcast_in_dim.22), channel_id=1, replica_groups=mesh['pix'=32,'feat'=8] {'pix'}, dimensions={0} | all-to-all | bytes 294912 | tf_op jit(solution)/shard_map/all_to_all | solution.py:77
  179.9 0.1 reshape.82
  180.0 0.3 fusion.44
  180.3 0.9 broadcast_in_dim.23
  181.2 7.0 %all-to-all-start.5 = ((bf16[8,64,512]{2,1,0:T(8,128)(2,1)}), bf16[8,64,512]{2,1,0:T(8,128)(2,1)S(1)}, u32[]{:S(2)}, u32[]{:S(2)}) async-start(bf16[8,64,512]{2,1,0:T(8,128)(2,1)} %broadcast_in_dim.23), calls=%async_computation.5 | async-start | bytes 1048576 | tf_op jit(solution)/shard_map/all_to_all | solution.py:82
  188.2 0.3 fusion.48
  188.4 0.2 collective-permute-start.17
  188.7 1.1 collective-permute-done.17
  189.7 1.2 collective-permute-start.18
  190.9 6.0 %collective-permute-done.18 = f32[64,64]{1,0:T(8,128)S(1)} collective-permute-done((f32[64,64]{1,0:T(8,128)S(1)}, f32[64,64]{1,0:T(8,128)S(1)}, u32[]{:S(2)}, u32[]{:S(2)}) %collective-permute-start.18) | collective-permute-done | bytes 16416 | tf_op jit(solution)/shard_map/ppermute | solution.py:89
  196.9 0.8 collective-permute-start.19
  197.8 5.0 %convolution_multiply_fusion = f32[1024,64]{0,1:T(8,128)S(1)} fusion(f32[1024,64]{0,1:T(8,128)S(1)} %fusion.12, bf16[64,4096]{1,0:T(8,128)(2,1)S(1)} %bitcast.37, bf16[1024,4096]{0,1:T(8,128)(2,1)} %bitcast.33), kind=kOutput, calls=%fused_computation.24 | convolution fusion | flops 536936448 | bytes 9437184 | tf_op jit(solution)/shard_map/dot_general | solution.py:159
  202.8 1.1 fusion.10
  (34 shorter events, 0.7 us)
Async XLA Ops:
  24.2 18.4 %copy-start = (f32[1024,64]{0,1:T(8,128)S(1)}, f32[1024,64]{0,1:T(8,128)}, u32[]{:S(2)}) copy-start(f32[1024,64]{0,1:T(8,128)} %param.10) | copy-start | bytes 786436
  43.0 62.6 %copy-start.2 = (f32[64,512]{1,0:T(8,128)S(1)}, f32[64,512]{1,0:T(8,128)}, u32[]{:S(2)}) copy-start(f32[64,512]{1,0:T(8,128)} %param.11) | copy-start | bytes 393220
  49.5 5.9 %collective-permute-start = (f32[64,576]{1,0:T(8,128)S(1)}, f32[64,576]{1,0:T(8,128)S(1)}, u32[]{:S(2)}, u32[]{:S(2)}) collective-permute-start(f32[64,576]{1,0:T(8,128)S(1)} %get-tuple-element.43), channel_id=1, source_target_pairs={{0,1},{1,2},{2,3},{3,4},{4,5},{5,6},{6,7},{7,0},{8,9},{9,10},{10,1... | collective-permute-start | bytes 442376 | tf_op jit(solution)/shard_map/ppermute | solution.py:41
  49.6 7.8 %collective-permute-start.1 = (f32[64,576]{1,0:T(8,128)S(1)}, f32[64,576]{1,0:T(8,128)S(1)}, u32[]{:S(2)}, u32[]{:S(2)}) collective-permute-start(f32[64,576]{1,0:T(8,128)S(1)} %get-tuple-element.44), channel_id=1, source_target_pairs={{0,2},{1,3},{2,4},{3,5},{4,6},{5,7},{6,0},{7,1},{8,10},{9,11},{10,... | collective-permute-start | bytes 442376 | tf_op jit(solution)/shard_map/ppermute | solution.py:41
  50.9 11.3 %collective-permute-start.2 = (f32[64,576]{1,0:T(8,128)S(1)}, f32[64,576]{1,0:T(8,128)S(1)}, u32[]{:S(2)}, u32[]{:S(2)}) collective-permute-start(f32[64,576]{1,0:T(8,128)S(1)} %get-tuple-element.45), channel_id=1, source_target_pairs={{0,3},{1,4},{2,5},{3,6},{4,7},{5,0},{6,1},{7,2},{8,11},{9,12},{10,... | collective-permute-start | bytes 442376 | tf_op jit(solution)/shard_map/ppermute | solution.py:41
  52.6 11.3 %collective-permute-start.3 = (f32[64,576]{1,0:T(8,128)S(1)}, f32[64,576]{1,0:T(8,128)S(1)}, u32[]{:S(2)}, u32[]{:S(2)}) collective-permute-start(f32[64,576]{1,0:T(8,128)S(1)} %get-tuple-element.46), channel_id=1, source_target_pairs={{0,4},{1,5},{2,6},{3,7},{4,0},{5,1},{6,2},{7,3},{8,12},{9,13},{10,... | collective-permute-start | bytes 442376 | tf_op jit(solution)/shard_map/ppermute | solution.py:41
  53.8 11.7 %collective-permute-start.4 = (f32[64,576]{1,0:T(8,128)S(1)}, f32[64,576]{1,0:T(8,128)S(1)}, u32[]{:S(2)}, u32[]{:S(2)}) collective-permute-start(f32[64,576]{1,0:T(8,128)S(1)} %get-tuple-element.47), channel_id=1, source_target_pairs={{0,5},{1,6},{2,7},{3,0},{4,1},{5,2},{6,3},{7,4},{8,13},{9,14},{10,... | collective-permute-start | bytes 442376 | tf_op jit(solution)/shard_map/ppermute | solution.py:41
  55.5 12.2 %collective-permute-start.5 = (f32[64,576]{1,0:T(8,128)S(1)}, f32[64,576]{1,0:T(8,128)S(1)}, u32[]{:S(2)}, u32[]{:S(2)}) collective-permute-start(f32[64,576]{1,0:T(8,128)S(1)} %get-tuple-element.48), channel_id=1, source_target_pairs={{0,6},{1,7},{2,0},{3,1},{4,2},{5,3},{6,4},{7,5},{8,14},{9,15},{10,... | collective-permute-start | bytes 442376 | tf_op jit(solution)/shard_map/ppermute | solution.py:41
  57.3 10.6 %collective-permute-start.6 = (f32[64,576]{1,0:T(8,128)S(1)}, f32[64,576]{1,0:T(8,128)S(1)}, u32[]{:S(2)}, u32[]{:S(2)}) collective-permute-start(f32[64,576]{1,0:T(8,128)S(1)} %get-tuple-element.49), channel_id=1, source_target_pairs={{0,7},{1,0},{2,1},{3,2},{4,3},{5,4},{6,5},{7,6},{8,15},{9,8},{10,9... | collective-permute-start | bytes 442376 | tf_op jit(solution)/shard_map/ppermute | solution.py:41
  106.7 14.4 %all-to-all-start.2 = ((bf16[8,64,512]{2,1,0:T(8,128)(2,1)}), bf16[8,64,512]{2,1,0:T(8,128)(2,1)S(1)}, u32[]{:S(2)}, u32[]{:S(2)}) async-start(bf16[8,64,512]{2,1,0:T(8,128)(2,1)} %broadcast_in_dim.21), calls=%async_computation.2 | async-start | bytes 1048576 | tf_op jit(solution)/shard_map/all_to_all | solution.py:82
  111.8 1.3 collective-permute-start.7
  113.1 7.1 %collective-permute-start.8 = (f32[64,64]{1,0:T(8,128)S(1)}, f32[64,64]{1,0:T(8,128)S(1)}, u32[]{:S(2)}, u32[]{:S(2)}) collective-permute-start(f32[64,64]{1,0:T(8,128)S(1)} %add.114), channel_id=1, source_target_pairs={{0,2},{1,3},{2,0},{3,1},{4,6},{5,7},{6,4},{7,5},{8,10},{9,11},{10,... | collective-permute-start | bytes 49160 | tf_op jit(solution)/shard_map/ppermute | solution.py:89
  120.2 6.0 %collective-permute-start.9 = (f32[64,64]{1,0:T(8,128)S(1)}, f32[64,64]{1,0:T(8,128)S(1)}, u32[]{:S(2)}, u32[]{:S(2)}) collective-permute-start(f32[64,64]{1,0:T(8,128)S(1)} %add.115), channel_id=1, source_target_pairs={{0,4},{1,5},{2,6},{3,7},{4,0},{5,1},{6,2},{7,3},{8,12},{9,13},{10,... | collective-permute-start | bytes 49160 | tf_op jit(solution)/shard_map/ppermute | solution.py:89
  121.1 5.6 %slice-start = ((s8[8388608]{0:T(1024)(128)(4,1)}), s8[4194304]{0:T(1024)(128)(4,1)S(1)}, s32[]{:S(2)}) async-start(s8[8388608]{0:T(1024)(128)(4,1)} %bitcast.34), calls=%async_computation.6 | async-start | bytes 8388608
  121.2 5.8 %slice-start.1 = ((s8[8388608]{0:T(1024)(128)(4,1)}), s8[4194304]{0:T(1024)(128)(4,1)S(1)}, s32[]{:S(2)}) async-start(s8[8388608]{0:T(1024)(128)(4,1)} %bitcast.34), calls=%async_computation.7 | async-start | bytes 8388608
  130.4 6.6 %collective-permute-start.10 = (f32[64,576]{1,0:T(8,128)S(1)}, f32[64,576]{1,0:T(8,128)S(1)}, u32[]{:S(2)}, u32[]{:S(2)}) collective-permute-start(f32[64,576]{1,0:T(8,128)S(1)} %get-tuple-element.36), channel_id=1, source_target_pairs={{0,1},{1,2},{2,3},{3,4},{4,5},{5,6},{6,7},{7,0},{8,9},{9,10},{10,1... | collective-permute-start | bytes 442376 | tf_op jit(solution)/shard_map/ppermute | solution.py:41
  130.4 8.4 %collective-permute-start.11 = (f32[64,576]{1,0:T(8,128)S(1)}, f32[64,576]{1,0:T(8,128)S(1)}, u32[]{:S(2)}, u32[]{:S(2)}) collective-permute-start(f32[64,576]{1,0:T(8,128)S(1)} %get-tuple-element.37), channel_id=1, source_target_pairs={{0,2},{1,3},{2,4},{3,5},{4,6},{5,7},{6,0},{7,1},{8,10},{9,11},{10,... | collective-permute-start | bytes 442376 | tf_op jit(solution)/shard_map/ppermute | solution.py:41
  131.5 12.7 %collective-permute-start.12 = (f32[64,576]{1,0:T(8,128)S(1)}, f32[64,576]{1,0:T(8,128)S(1)}, u32[]{:S(2)}, u32[]{:S(2)}) collective-permute-start(f32[64,576]{1,0:T(8,128)S(1)} %get-tuple-element.38), channel_id=1, source_target_pairs={{0,3},{1,4},{2,5},{3,6},{4,7},{5,0},{6,1},{7,2},{8,11},{9,12},{10,... | collective-permute-start | bytes 442376 | tf_op jit(solution)/shard_map/ppermute | solution.py:41
  134.0 11.4 %collective-permute-start.13 = (f32[64,576]{1,0:T(8,128)S(1)}, f32[64,576]{1,0:T(8,128)S(1)}, u32[]{:S(2)}, u32[]{:S(2)}) collective-permute-start(f32[64,576]{1,0:T(8,128)S(1)} %get-tuple-element.39), channel_id=1, source_target_pairs={{0,4},{1,5},{2,6},{3,7},{4,0},{5,1},{6,2},{7,3},{8,12},{9,13},{10,... | collective-permute-start | bytes 442376 | tf_op jit(solution)/shard_map/ppermute | solution.py:41
  134.3 11.7 %collective-permute-start.14 = (f32[64,576]{1,0:T(8,128)S(1)}, f32[64,576]{1,0:T(8,128)S(1)}, u32[]{:S(2)}, u32[]{:S(2)}) collective-permute-start(f32[64,576]{1,0:T(8,128)S(1)} %get-tuple-element.40), channel_id=1, source_target_pairs={{0,5},{1,6},{2,7},{3,0},{4,1},{5,2},{6,3},{7,4},{8,13},{9,14},{10,... | collective-permute-start | bytes 442376 | tf_op jit(solution)/shard_map/ppermute | solution.py:41
  137.0 12.2 %collective-permute-start.15 = (f32[64,576]{1,0:T(8,128)S(1)}, f32[64,576]{1,0:T(8,128)S(1)}, u32[]{:S(2)}, u32[]{:S(2)}) collective-permute-start(f32[64,576]{1,0:T(8,128)S(1)} %get-tuple-element.41), channel_id=1, source_target_pairs={{0,6},{1,7},{2,0},{3,1},{4,2},{5,3},{6,4},{7,5},{8,14},{9,15},{10,... | collective-permute-start | bytes 442376 | tf_op jit(solution)/shard_map/ppermute | solution.py:41
  138.8 10.4 %collective-permute-start.16 = (f32[64,576]{1,0:T(8,128)S(1)}, f32[64,576]{1,0:T(8,128)S(1)}, u32[]{:S(2)}, u32[]{:S(2)}) collective-permute-start(f32[64,576]{1,0:T(8,128)S(1)} %get-tuple-element.42), channel_id=1, source_target_pairs={{0,7},{1,0},{2,1},{3,2},{4,3},{5,4},{6,5},{7,6},{8,15},{9,8},{10,9... | collective-permute-start | bytes 442376 | tf_op jit(solution)/shard_map/ppermute | solution.py:41
  180.3 22.4 %copy-start.1 = (f32[64,512]{1,0:T(8,128)}, f32[64,512]{1,0:T(8,128)S(1)}, u32[]{:S(2)}) copy-start(f32[64,512]{1,0:T(8,128)S(1)} %get-tuple-element.53) | copy-start | bytes 393220
  181.2 16.5 %all-to-all-start.5 = ((bf16[8,64,512]{2,1,0:T(8,128)(2,1)}), bf16[8,64,512]{2,1,0:T(8,128)(2,1)S(1)}, u32[]{:S(2)}, u32[]{:S(2)}) async-start(bf16[8,64,512]{2,1,0:T(8,128)(2,1)} %broadcast_in_dim.23), calls=%async_computation.5 | async-start | bytes 1048576 | tf_op jit(solution)/shard_map/all_to_all | solution.py:82
  188.4 1.3 collective-permute-start.17
  189.7 7.1 %collective-permute-start.18 = (f32[64,64]{1,0:T(8,128)S(1)}, f32[64,64]{1,0:T(8,128)S(1)}, u32[]{:S(2)}, u32[]{:S(2)}) collective-permute-start(f32[64,64]{1,0:T(8,128)S(1)} %add.127), channel_id=1, source_target_pairs={{0,2},{1,3},{2,0},{3,1},{4,6},{5,7},{6,4},{7,5},{8,10},{9,11},{10,... | collective-permute-start | bytes 49160 | tf_op jit(solution)/shard_map/ppermute | solution.py:89
  196.9 5.9 %collective-permute-start.19 = (f32[64,64]{1,0:T(8,128)S(1)}, f32[64,64]{1,0:T(8,128)S(1)}, u32[]{:S(2)}, u32[]{:S(2)}) collective-permute-start(f32[64,64]{1,0:T(8,128)S(1)} %add.128), channel_id=1, source_target_pairs={{0,4},{1,5},{2,6},{3,7},{4,0},{5,1},{6,2},{7,3},{8,12},{9,13},{10,... | collective-permute-start | bytes 49160 | tf_op jit(solution)/shard_map/ppermute | solution.py:89
